TPU v7x, 128 devices: a whole 4x4x4 slice. The times are simulated.
128 devices in a mesh: shard: 32 (over x, y, core), tensor: 4 (over z).
Axes of the slice: x: 4, y: 4, z: 4, core: 2. Of those that a mesh axis runs over, the one named last changes fastest.
Arguments:
- grads: bfloat16 [384, 256, 256], P('shard', 'tensor'), may hold values from -60 to 60
- owner: int32 [384], replicated, may hold values from 0 to 31, as said below
- slot: int32 [384], replicated, may hold values from 0 to 23, as said below
- stat_left: float32 [768, 256, 256], P('shard', 'tensor'), may hold values from -144 to 2704, as said below
- stat_right: float32 [768, 256, 256], P('shard', 'tensor'), may hold values from -144 to 2704, as said below
- root_left: float32 [768, 256, 256], P('shard', 'tensor'), may hold values from -0.72 to 2.72, as said below
- root_right: float32 [768, 256, 256], P('shard'), may hold values from -0.72 to 2.72, as said below
- moment: float32 [768, 256, 256], P('shard', 'tensor'), may hold values from 0.1 to 10
- momentum: float32 [768, 256, 256], P('shard', 'tensor'), may hold values from -6 to 6
- master: float32 [768, 256, 256], P('shard', 'tensor'), may hold values from -0.3 to 0.3
Outputs:
- stat_left_new: float32 [768, 256, 256], P('shard', 'tensor')
- stat_right_new: float32 [768, 256, 256], P('shard', 'tensor')
- moment_new: float32 [768, 256, 256], P('shard', 'tensor')
- momentum_new: float32 [768, 256, 256], P('shard', 'tensor')
- master_new: float32 [768, 256, 256], P('shard', 'tensor')
- weights_new: bfloat16 [384, 256, 256], P('shard', 'tensor')
Inputs may be any that keep to these rules, and one draw needn't show every extreme that they name: Each owner group holds at most 24 blocks, some exactly 24; no owner group holds two blocks of one shard group (blocks b with equal b // 12). `slot`: the blocks of one owner group have distinct slots. `stat_left`: Symmetric. `stat_right`: Symmetric. `root_left`: Symmetric. `root_right`: Symmetric.
All inputs are finite; a program needn't handle non-finite values.
Results may differ from a plain program's by a relative error of at most 0.001.
Values may be sent and summed in bfloat16 or wider, within the bound.
No kernel may reach another device: no remote copies, remote signals or barrier semaphores. Data moves between devices by JAX's collectives and lax.ppermute only.
A program may use at most 128 MiB of HBM per device.

v0:
```python
import jax
import jax.numpy as jnp
from jax import lax
from jax.sharding import PartitionSpec as P

beta_stat = 0.95
beta_mom = 0.9
learn_rate = 0.01
eps_root = 1e-08
eps_mean = 1e-06


def on_device(
    grads, owner, slot, stat_left, stat_right, root_left, root_right, moment, momentum, master
):
    groups = lax.axis_size("shard")
    splits = lax.axis_size("tensor")
    slots_dev = stat_left.shape[0]
    rows_dev = stat_left.shape[1]
    order = stat_left.shape[2]
    blocks_group = grads.shape[0]
    shard_index = lax.axis_index("shard")
    tensor_index = lax.axis_index("tensor")
    owner_grid = owner.reshape(groups, blocks_group)
    slot_grid = slot.reshape(groups, blocks_group)
    local_owner = lax.dynamic_index_in_dim(owner_grid, shard_index, 0, keepdims=False)
    hit_mask = owner_grid == shard_index
    slot_ids = jnp.arange(slots_dev, dtype=jnp.int32)
    select = jnp.sum(
        (slot_grid[None, :, :] == slot_ids[:, None, None]) & hit_mask[None, :, :], axis=2
    ).astype(jnp.bfloat16)
    group_ids = jnp.arange(groups, dtype=jnp.int32)
    picker = (local_owner[None, :] == group_ids[:, None]).astype(jnp.bfloat16)
    row_start = tensor_index * rows_dev
    whole_rows = lax.all_gather(grads, "tensor", axis=1, tiled=True)
    outgoing = jnp.einsum(
        "gi,ixy->gxy", picker, whole_rows, preferred_element_type=jnp.float32
    ).astype(jnp.bfloat16)
    arrived = lax.all_to_all(outgoing, "shard", split_axis=0, concat_axis=0, tiled=True)
    grad_whole = jnp.einsum(
        "kg,gxy->kxy", select, arrived, preferred_element_type=jnp.float32
    ).astype(jnp.bfloat16)
    grad_piece = lax.dynamic_slice_in_dim(grad_whole, row_start, rows_dev, 1)
    highest = lax.Precision.HIGHEST
    grad_full = grad_whole.astype(jnp.float32)
    grad_rows = grad_piece.astype(jnp.float32)
    grad_cols = lax.dynamic_slice_in_dim(grad_full, row_start, rows_dev, 2)
    left_new = beta_stat * stat_left + (1.0 - beta_stat) * jnp.einsum(
        "kij,klj->kil", grad_rows, grad_full, precision=highest
    )
    right_new = beta_stat * stat_right + (1.0 - beta_stat) * jnp.einsum(
        "kji,kjl->kil", grad_cols, grad_full, precision=highest
    )
    second_new = beta_stat * moment + (1.0 - beta_stat) * grad_rows * grad_rows
    adam_step = grad_rows / (jnp.sqrt(second_new) + eps_root)
    precond = jnp.einsum("kij,kjl->kil", root_left, grad_full, precision=highest)
    precond = jnp.einsum("kij,kjl->kil", precond, root_right, precision=highest)
    adam_sum, precond_sum = lax.psum(
        (jnp.sum(adam_step * adam_step, axis=(1, 2)), jnp.sum(precond * precond, axis=(1, 2))),
        "tensor",
    )
    entries = float(rows_dev * splits * order)
    scale_ratio = jnp.sqrt(adam_sum / entries + eps_mean) / jnp.sqrt(
        precond_sum / entries + eps_mean
    )
    velocity_new = beta_mom * momentum + (1.0 - beta_mom) * scale_ratio[:, None, None] * precond
    weight_new = master - learn_rate * velocity_new
    weight_half = weight_new.astype(jnp.bfloat16)
    returning = jnp.einsum(
        "kg,kxy->gxy", select, weight_half, preferred_element_type=jnp.float32
    ).astype(jnp.bfloat16)
    back_rows = lax.all_to_all(returning, "shard", split_axis=0, concat_axis=0, tiled=True)
    weights_local = jnp.take(back_rows, local_owner, axis=0)
    return (left_new, right_new, second_new, velocity_new, weight_new, weights_local)


def solution(mesh):
    placed = (
        P("shard", "tensor", None),
        P(),
        P(),
        P("shard", "tensor", None),
        P("shard", "tensor", None),
        P("shard", "tensor", None),
        P("shard", None, None),
        P("shard", "tensor", None),
        P("shard", "tensor", None),
        P("shard", "tensor", None),
    )
    return jax.shard_map(
        on_device,
        mesh=mesh,
        in_specs=placed,
        out_specs=(
            P("shard", "tensor", None),
            P("shard", "tensor", None),
            P("shard", "tensor", None),
            P("shard", "tensor", None),
            P("shard", "tensor", None),
            P("shard", "tensor", None),
        ),
        check_vma=False,
    )
```

profile of v0, /device:TPU:1, one launch (start us, length us, event | category | flops | bytes accessed | tf_op | source)
XLA Modules:
  0.0 176.2 jit_solution(17148994907368642026)
XLA Ops:
  7.2 0.7 all-gather.2.cloned.1.call-update
  7.9 0.8 reshape.57
  8.7 30.7 %all-gather.2.cloned.1.call-done = bf16[12,256,256]{2,1,0:T(8,128)(2,1)} async-done(((bf16[12,64,256]{2,1,0:T(8,128)(2,1)}), bf16[12,256,256]{2,1,0:T(8,128)(2,1)}) %all-gather.2.cloned.1.call-update) | async-done | bytes 1572880 | tf_op jit(solution)/shard_map/all_gather | solution.py:35
  39.4 2.8 %convolution_convert_fusion = bf16[32,256,256]{2,0,1:T(8,128)(2,1)S(1)} fusion(bf16[12,256,256]{2,1,0:T(8,128)(2,1)} %all-gather.2.cloned.1.call-done, s32[12]{0:T(128)S(1)} %get-tuple-element.39), kind=kOutput, calls=%fused_computation.3 | convolution fusion | flops 52429184 | bytes 5767216 | tf_op jit(solution)/shard_map/gi,ixy->gxy/dot_general | solution.py:36
  42.2 4.4 %copy.84 = bf16[32,256,256]{2,1,0:T(8,128)(2,1)} copy(bf16[32,256,256]{2,0,1:T(8,128)(2,1)S(1)} %convolution_convert_fusion) | data formatting | bytes 8388608 | tf_op jit(solution)/shard_map/convert_element_type | solution.py:38
  46.6 8.1 %all-to-all-start = ((bf16[32,256,256]{2,1,0:T(8,128)(2,1)}), bf16[32,256,256]{2,1,0:T(8,128)(2,1)}, u32[]{:S(2)}, u32[]{:S(2)}) async-start(bf16[32,256,256]{2,1,0:T(8,128)(2,1)} %copy.84), calls=%async_computation | async-start | bytes 8388608 | tf_op jit(solution)/shard_map/all_to_all | solution.py:39
  55.0 51.6 %all-to-all-done = bf16[32,256,256]{2,1,0:T(8,128)(2,1)} async-done(((bf16[32,256,256]{2,1,0:T(8,128)(2,1)}), bf16[32,256,256]{2,1,0:T(8,128)(2,1)}, u32[]{:S(2)}, u32[]{:S(2)}) %all-to-all-start) | async-done | bytes 4194336 | tf_op jit(solution)/shard_map/all_to_all | solution.py:39
  106.6 4.7 %fusion.8 = bf16[24,256,256]{2,0,1:T(8,128)(2,1)S(1)} fusion(bf16[32,256,256]{2,1,0:T(8,128)(2,1)} %all-to-all-done, s32[24,32]{1,0:T(8,128)S(1)} %convert_reduce_fusion), kind=kOutput, calls=%fused_computation.11 | convolution fusion | flops 102236928 | bytes 7343104 | tf_op jit(solution)/shard_map/kg,gxy->kxy/dot_general | solution.py:40
  111.3 0.5 constant_dynamic-slice_fusion
  111.8 2.0 %copy-done.3 = f32[24,64,256]{2,1,0:T(8,128)S(1)} copy-done((f32[24,64,256]{2,1,0:T(8,128)S(1)}, f32[24,64,256]{2,1,0:T(8,128)}, u32[]{:S(2)}) %copy-start.3) | copy-done | bytes 1572888
  113.8 1.5 fusion.17
  115.3 0.8 fusion.4
  116.1 0.6 copy-done.4
  116.7 1.8 %fusion.14 = f32[24,64,256]{2,0,1:T(8,128)S(1)} fusion(f32[24,64,256]{2,1,0:T(8,128)S(1)} %fusion.4, f32[24,64,256]{2,1,0:T(8,128)S(1)} %copy-done.4), kind=kLoop, calls=%fused_computation.18 | loop fusion | flops 1179648 | bytes 4718592 | tf_op jit(solution)/shard_map/add | solution.py:51
  118.5 1.6 copy.98
  120.2 2.0 %fusion.2 = f32[24,256,64]{1,2,0:T(8,128)S(1)} fusion(f32[24,64,256]{2,1,0:T(8,128)S(1)} %copy-done, bf16[24,256,256]{2,0,1:T(8,128)(2,1)S(1)} %fusion.8), kind=kOutput, calls=%fused_computation.4 | convolution fusion | flops 1207959552 | bytes 6291456 | tf_op jit(solution)/shard_map/kij,kjl->kil/dot_general | solution.py:56
  122.2 5.3 %multiply_reduce_fusion = (f32[24]{0:T(128)S(1)}, f32[24,64,256]{2,1,0:T(8,128)}) fusion(f32[24,256,64]{1,2,0:T(8,128)S(1)} %fusion.2, f32[24,256,256]{2,1,0:T(8,128)S(1)} %bitcast.19), kind=kOutput, calls=%fused_computation.26 | convolution fusion | flops 1208745984 | bytes 9437280 | tf_op jit(solution)/shard_map/kij,kjl->kil/dot_general | solution.py:57
  127.5 7.4 %all-reduce = (f32[24]{0:T(128)S(1)}, f32[24]{0:T(128)S(1)}) all-reduce(f32[24]{0:T(128)S(1)} %get-tuple-element.45, f32[24]{0:T(128)S(1)} %get-tuple-element.43), channel_id=1, replica_groups=mesh['shard'=32,'tensor'=4] {'tensor'}, use_global_device_ids=true, to_apply=%region_4.5 | all-reduce | flops 48 | bytes 384 | tf_op jit(solution)/shard_map/psum | solution.py:58
  134.9 4.8 %fusion.31 = (bf16[24,64,256]{2,1,0:T(8,128)(2,1)S(1)}, f32[24,64,256]{2,1,0:T(8,128)}, f32[24,64,256]{2,1,0:T(8,128)}) fusion(f32[24,64,256]{2,1,0:T(8,128)} %param.19, f32[24,64,256]{2,1,0:T(8,128)} %get-tuple-element.46, f32[24]{0:T(128)S(1)} %multiply_multiply_fusion.1, f32[24,64,256]{2,1,0:T(8,128)} %param.18), kind=kLoop, calls=%fused_computation.53 | loop fusion | flops 2359296 | bytes 8650848 | tf_op jit(solution)/shard_map/convert_element_type | solution.py:68
  139.7 0.7 convolution_convert_fusion.1
  140.4 1.6 copy.96
  142.0 9.1 %all-to-all-start.1 = ((bf16[32,64,256]{2,1,0:T(8,128)(2,1)}), bf16[32,64,256]{2,1,0:T(8,128)(2,1)S(1)}, u32[]{:S(2)}, u32[]{:S(2)}) async-start(bf16[32,64,256]{2,1,0:T(8,128)(2,1)} %copy.96), calls=%async_computation.1 | async-start | bytes 2097152 | tf_op jit(solution)/shard_map/all_to_all | solution.py:72
  151.1 2.5 %fusion.13 = f32[24,64,256]{2,0,1:T(8,128)S(1)} fusion(bf16[24,64,256]{2,0,1:T(8,128)(2,1)S(1)} %get-tuple-element.44, f32[24,64,256]{2,1,0:T(8,128)} %param.17), kind=kLoop, calls=%fused_computation.15 | loop fusion | flops 1966080 | bytes 3932160 | tf_op jit(solution)/shard_map/add | solution.py:54
  153.5 1.6 copy.99
  155.2 0.8 copy-done.2
  156.0 1.1 fusion.6
  157.1 0.3 copy-done.5
  157.4 1.8 %fusion.16 = f32[24,64,256]{2,0,1:T(8,128)S(1)} fusion(f32[24,64,256]{2,1,0:T(8,128)S(1)} %fusion.6, f32[24,64,256]{2,1,0:T(8,128)S(1)} %copy-done.5), kind=kLoop, calls=%fused_computation.22 | loop fusion | flops 1179648 | bytes 4718592 | tf_op jit(solution)/shard_map/add | solution.py:48
  159.2 1.6 copy.97
  160.9 7.1 %all-to-all-done.1 = bf16[32,64,256]{2,1,0:T(8,128)(2,1)S(1)} async-done(((bf16[32,64,256]{2,1,0:T(8,128)(2,1)}), bf16[32,64,256]{2,1,0:T(8,128)(2,1)S(1)}, u32[]{:S(2)}, u32[]{:S(2)}) %all-to-all-start.1) | async-done | bytes 1048608 | tf_op jit(solution)/shard_map/all_to_all | solution.py:72
  168.0 0.6 gather_fusion
  168.5 0.9 broadcast_select_fusion
  (25 shorter events, 0.4 us)
Async XLA Ops:
  7.2 113.0 %copy-start = (f32[24,64,256]{2,1,0:T(8,128)S(1)}, f32[24,64,256]{2,1,0:T(8,128)}, u32[]{:S(2)}) copy-start(f32[24,64,256]{2,1,0:T(8,128)} %param.15) | copy-start | bytes 4718596
  7.2 32.2 %all-gather.2.cloned.1.call-start = ((), (), s32[]{:S(2)}) async-start(), calls=%async_computation.2 | async-start | bytes 1966080 | tf_op jit(solution)/shard_map/all_gather | solution.py:35
  46.6 8.2 %copy-start.6 = (s32[384]{0:T(512)S(1)}, s32[384]{0:T(512)}, u32[]{:S(2)}) copy-start(s32[384]{0:T(512)} %param.12) | copy-start | bytes 4612
  46.6 60.0 %all-to-all-start = ((bf16[32,256,256]{2,1,0:T(8,128)(2,1)}), bf16[32,256,256]{2,1,0:T(8,128)(2,1)}, u32[]{:S(2)}, u32[]{:S(2)}) async-start(bf16[32,256,256]{2,1,0:T(8,128)(2,1)} %copy.84), calls=%async_computation | async-start | bytes 8388608 | tf_op jit(solution)/shard_map/all_to_all | solution.py:39
  111.2 8.9 %copy-start.1 = (bf16[24,256,256]{2,0,1:T(8,128)(2,1)}, bf16[24,256,256]{2,0,1:T(8,128)(2,1)S(1)}, u32[]{:S(2)}) copy-start(bf16[24,256,256]{2,0,1:T(8,128)(2,1)S(1)} %fusion.8) | copy-start | bytes 9437188
  111.3 2.5 %copy-start.3 = (f32[24,64,256]{2,1,0:T(8,128)S(1)}, f32[24,64,256]{2,1,0:T(8,128)}, u32[]{:S(2)}) copy-start(f32[24,64,256]{2,1,0:T(8,128)} %param.17) | copy-start | bytes 4718596
  115.3 1.4 copy-start.4
  116.7 5.5 %slice-start = ((s8[6291456]{0:T(1024)(128)(4,1)}), s8[4194304]{0:T(1024)(128)(4,1)S(1)}, s32[]{:S(2)}) async-start(s8[6291456]{0:T(1024)(128)(4,1)} %bitcast.18), calls=%async_computation.3 | async-start | bytes 8388608
  118.5 3.6 %slice-start.1 = ((s8[6291456]{0:T(1024)(128)(4,1)}), s8[2097152]{0:T(1024)(128)(4,1)S(1)}, s32[]{:S(2)}) async-start(s8[6291456]{0:T(1024)(128)(4,1)} %bitcast.18), calls=%async_computation.4 | async-start | bytes 4194304
  142.0 26.0 %all-to-all-start.1 = ((bf16[32,64,256]{2,1,0:T(8,128)(2,1)}), bf16[32,64,256]{2,1,0:T(8,128)(2,1)S(1)}, u32[]{:S(2)}, u32[]{:S(2)}) async-start(bf16[32,64,256]{2,1,0:T(8,128)(2,1)} %copy.96), calls=%async_computation.1 | async-start | bytes 2097152 | tf_op jit(solution)/shard_map/all_to_all | solution.py:72
  153.5 2.5 %copy-start.2 = (bf16[24,256,256]{2,0,1:T(8,128)(2,1)S(1)}, bf16[24,256,256]{2,0,1:T(8,128)(2,1)}, u32[]{:S(2)}) copy-start(bf16[24,256,256]{2,0,1:T(8,128)(2,1)} %copy-done.1) | copy-start | bytes 9437188
  156.0 1.4 copy-start.5
Sparse Core Ops, SparseCore 0:
  9.7 29.6 all-gather.1
where the time goes:
time: 177 us; the launch traced here: 176 us
  waiting for transfers between devices  90 us (51%)
  matrix products  17.3 us (10%)
  starting transfers between devices  17.2 us (10%)
  local copies, waits for them, and re-layouts  16.8 us (9%)
  between operations  14.2 us (8%)
  other arithmetic  13.4 us (8%)
  blocking collectives  7.38 us (4%)
    all_to_all x1, waiting for transfers between devices, on_device(): lax.all_to_all(outgoing, 'shard', split_axis=0, concat_axis=0, tiled=True)  51.6 us
    all_gather x1, waiting for transfers between devices, on_device(): whole_rows = lax.all_gather(grads, 'tensor', axis=1, tiled=True)  30.7 us
    all_to_all x1, starting transfers between devices, on_device(): lax.all_to_all(returning, 'shard', split_axis=0, concat_axis=0, tiled=True)  9.05 us
    unnamed x21, local copies, waits for them, and re-layouts  8.7 us
    all_to_all x1, starting transfers between devices, on_device(): lax.all_to_all(outgoing, 'shard', split_axis=0, concat_axis=0, tiled=True)  8.06 us
    psum x1, blocking collectives, on_device(): lax.psum((jnp.sum(adam_step * adam_step, axis=(1, 2)), jnp.sum(precond *...  7.38 us
    all_to_all x1, waiting for transfers between devices, on_device(): lax.all_to_all(returning, 'shard', split_axis=0, concat_axis=0, tiled=True)  7.11 us
    dot_general x1, matrix products, on_device(): precond = jnp.einsum('kij,kjl->kil', precond, root_right, precision=highest)  5.35 us
  transfers between devices with their start and end apart: 3, of which 3 were waited for; matrix products, arithmetic and copies ran while one was open for 6% of the time, Pallas kernels for 0%

commit v1 on v0

--- a/solution.py
+++ b/solution.py
@@ -8,6 +8,31 @@
 learn_rate = 0.01
 eps_root = 1e-08
 eps_mean = 1e-06
+
+
+def split3(x):
+    hi = x.astype(jnp.bfloat16)
+    rest = x - hi.astype(jnp.float32)
+    mid = rest.astype(jnp.bfloat16)
+    lo = (rest - mid.astype(jnp.float32)).astype(jnp.bfloat16)
+    return hi, mid, lo
+
+
+def gather_rows(piece, splits, tensor_index):
+    right = [(i, (i + 1) % splits) for i in range(splits)]
+    left = [(i, (i - 1) % splits) for i in range(splits)]
+    from_left = lax.ppermute(piece, "tensor", right)
+    from_right = lax.ppermute(piece, "tensor", left)
+    half = piece.shape[0] // 2
+    far_a = lax.ppermute(from_left[:half], "tensor", right)
+    far_b = lax.ppermute(from_right[half:], "tensor", left)
+    far = jnp.concatenate([far_a, far_b], 0)
+    rows = piece.shape[1]
+    whole = jnp.zeros((piece.shape[0], rows * splits, piece.shape[2]), piece.dtype)
+    for shift, part in ((0, piece), (1, from_right), (2, far), (splits - 1, from_left)):
+        start = ((tensor_index + shift) % splits) * rows
+        whole = lax.dynamic_update_slice_in_dim(whole, part, start, 1)
+    return whole
 
 
 def on_device(
@@ -32,28 +57,32 @@
     group_ids = jnp.arange(groups, dtype=jnp.int32)
     picker = (local_owner[None, :] == group_ids[:, None]).astype(jnp.bfloat16)
     row_start = tensor_index * rows_dev
-    whole_rows = lax.all_gather(grads, "tensor", axis=1, tiled=True)
     outgoing = jnp.einsum(
-        "gi,ixy->gxy", picker, whole_rows, preferred_element_type=jnp.float32
+        "gi,ixy->gxy", picker, grads, preferred_element_type=jnp.float32
     ).astype(jnp.bfloat16)
     arrived = lax.all_to_all(outgoing, "shard", split_axis=0, concat_axis=0, tiled=True)
-    grad_whole = jnp.einsum(
+    grad_piece = jnp.einsum(
         "kg,gxy->kxy", select, arrived, preferred_element_type=jnp.float32
     ).astype(jnp.bfloat16)
-    grad_piece = lax.dynamic_slice_in_dim(grad_whole, row_start, rows_dev, 1)
+    grad_whole = gather_rows(grad_piece, splits, tensor_index)
     highest = lax.Precision.HIGHEST
-    grad_full = grad_whole.astype(jnp.float32)
-    grad_rows = grad_piece.astype(jnp.float32)
-    grad_cols = lax.dynamic_slice_in_dim(grad_full, row_start, rows_dev, 2)
+    f32 = jnp.float32
+    grad_cols = lax.dynamic_slice_in_dim(grad_whole, row_start, rows_dev, 2)
     left_new = beta_stat * stat_left + (1.0 - beta_stat) * jnp.einsum(
-        "kij,klj->kil", grad_rows, grad_full, precision=highest
+        "kij,klj->kil", grad_piece, grad_whole, preferred_element_type=f32
     )
     right_new = beta_stat * stat_right + (1.0 - beta_stat) * jnp.einsum(
-        "kji,kjl->kil", grad_cols, grad_full, precision=highest
+        "kji,kjl->kil", grad_cols, grad_whole, preferred_element_type=f32
     )
+    grad_rows = grad_piece.astype(f32)
     second_new = beta_stat * moment + (1.0 - beta_stat) * grad_rows * grad_rows
     adam_step = grad_rows / (jnp.sqrt(second_new) + eps_root)
-    precond = jnp.einsum("kij,kjl->kil", root_left, grad_full, precision=highest)
+    root_hi, root_mid, root_lo = split3(root_left)
+    precond = (
+        jnp.einsum("kij,kjl->kil", root_hi, grad_whole, preferred_element_type=f32)
+        + jnp.einsum("kij,kjl->kil", root_mid, grad_whole, preferred_element_type=f32)
+        + jnp.einsum("kij,kjl->kil", root_lo, grad_whole, preferred_element_type=f32)
+    )
     precond = jnp.einsum("kij,kjl->kil", precond, root_right, precision=highest)
     adam_sum, precond_sum = lax.psum(
         (jnp.sum(adam_step * adam_step, axis=(1, 2)), jnp.sum(precond * precond, axis=(1, 2))),

time: 177 us -> 195 us (1.10)
  local copies, waits for them, and re-layouts: 16.8 us -> 85.9 us
  waiting for transfers between devices: 90 us -> 40.2 us
  between operations: 14.2 us -> 0.92 us
  starting transfers between devices: 17.2 us -> 23.5 us
  blocking collectives: 7.38 us -> 9.41 us
    dynamic_update_slice x0 -> x4, local copies, waits for them, and re-layouts: none -> 61.5 us  [gather_rows(): whole = lax.dynamic_update_slice_in_dim(whole, part, start, 1)]
    all_to_all x1, waiting for transfers between devices: 51.6 us -> 16.6 us  [on_device(): lax.all_to_all(outgoing, 'shard', split_axis=0, concat_axis=0, tiled=True)]
    all_gather x1 -> x0, waiting for transfers between devices: 30.7 us -> none  [on_device(): whole_rows = lax.all_gather(grads, 'tensor', axis=1, tiled=True)]
    ppermute x0 -> x4, waiting for transfers between devices: none -> 16.8 us  [the longest x1 16.8 us: gather_rows(): from_right = lax.ppermute(piece, 'tensor', left)]
    ppermute x0 -> x4, starting transfers between devices: none -> 7.17 us  [the longest x1 3.76 us: gather_rows(): from_right = lax.ppermute(piece, 'tensor', left)]
    ppermute x0 -> x2, local copies, waits for them, and re-layouts: none -> 5.01 us  [the longest x1 2.5 us: gather_rows(): from_right = lax.ppermute(piece, 'tensor', left)]
    unnamed x21 -> x23, local copies, waits for them, and re-layouts: 8.7 us -> 6.15 us
    concatenate x0 -> x1, local copies, waits for them, and re-layouts: none -> 2.5 us  [gather_rows(): far = jnp.concatenate([far_a, far_b], 0)]
  transfers between devices with their start and end apart: 3 -> 6, of which waited for: 3 -> 3; matrix products, arithmetic and copies ran while one was open for 6% -> 27% of each run, Pallas kernels for 0% -> 0%
where the time goes in v1:
time: 195 us; the launch traced here: 193 us
  local copies, waits for them, and re-layouts  85.9 us (44%)
  waiting for transfers between devices  40.2 us (21%)
  starting transfers between devices  23.5 us (12%)
  matrix products  18.5 us (9%)
  other arithmetic  14.8 us (8%)
  blocking collectives  9.41 us (5%)
    dynamic_update_slice x4, local copies, waits for them, and re-layouts, gather_rows(): whole = lax.dynamic_update_slice_in_dim(whole, part, start, 1)  61.5 us
    ppermute x1, waiting for transfers between devices, gather_rows(): from_right = lax.ppermute(piece, 'tensor', left)  16.8 us
    all_to_all x1, waiting for transfers between devices, on_device(): lax.all_to_all(outgoing, 'shard', split_axis=0, concat_axis=0, tiled=True)  16.6 us
    psum x1, blocking collectives, on_device(): lax.psum((jnp.sum(adam_step * adam_step, axis=(1, 2)), jnp.sum(precond *...  9.41 us
    all_to_all x1, starting transfers between devices, on_device(): lax.all_to_all(outgoing, 'shard', split_axis=0, concat_axis=0, tiled=True)  8.58 us
    all_to_all x1, starting transfers between devices, on_device(): lax.all_to_all(returning, 'shard', split_axis=0, concat_axis=0, tiled=True)  7.79 us
    all_to_all x1, waiting for transfers between devices, on_device(): lax.all_to_all(returning, 'shard', split_axis=0, concat_axis=0, tiled=True)  6.84 us
    unnamed x23, local copies, waits for them, and re-layouts  6.15 us
  transfers between devices with their start and end apart: 6, of which 3 were waited for; matrix products, arithmetic and copies ran while one was open for 27% of the time, Pallas kernels for 0%

profile of v1, /device:TPU:1, one launch (start us, length us, event | category | flops | bytes accessed | tf_op | source)
XLA Modules:
  0.0 193.3 jit_solution(7644994353711956710)
XLA Ops:
  2.6 1.6 copy.77
  4.1 8.6 %all-to-all-start = ((bf16[32,64,256]{2,1,0:T(8,128)(2,1)}), bf16[32,64,256]{2,1,0:T(8,128)(2,1)S(1)}, u32[]{:S(2)}, u32[]{:S(2)}) async-start(bf16[32,64,256]{2,1,0:T(8,128)(2,1)} %copy.77), calls=%async_computation | async-start | bytes 2097152 | tf_op jit(solution)/shard_map/all_to_all | solution.py:63
  13.1 16.6 %all-to-all-done = bf16[32,64,256]{2,1,0:T(8,128)(2,1)S(1)} async-done(((bf16[32,64,256]{2,1,0:T(8,128)(2,1)}), bf16[32,64,256]{2,1,0:T(8,128)(2,1)S(1)}, u32[]{:S(2)}, u32[]{:S(2)}) %all-to-all-start) | async-done | bytes 1048608 | tf_op jit(solution)/shard_map/all_to_all | solution.py:63
  29.6 3.9 %fusion.7 = (f32[24]{0:T(128)}, f32[24,64,256]{2,0,1:T(8,128)S(1)}, bf16[24,64,256]{2,0,1:T(8,128)(2,1)S(1)}) fusion(f32[24,64,256]{2,1,0:T(8,128)} %param.17, bf16[32,64,256]{2,1,0:T(8,128)(2,1)S(1)} %all-to-all-done, s32[24,32]{1,0:T(8,128)S(1)} %convert_reduce_fusion), kind=kOutput, calls=%fused_computation.20 | convolution fusion | flops 29098728 | bytes 4983904 | tf_op jit(solution)/shard_map/kg,gxy->kxy/dot_general | solution.py:64
  33.5 3.8 %collective-permute-start = (bf16[24,64,256]{2,0,1:T(8,128)(2,1)S(1)}, bf16[24,64,256]{2,0,1:T(8,128)(2,1)S(1)}, u32[]{:S(2)}, u32[]{:S(2)}) collective-permute-start(bf16[24,64,256]{2,0,1:T(8,128)(2,1)S(1)} %get-tuple-element.39), channel_id=1, source_target_pairs={{0,3},{1,0},{2,1},{3,2},{4,7},{5,4},{6,5},{7,6},{8,11},{9,8},{10,9... | collective-permute-start | bytes 2359304 | tf_op jit(solution)/shard_map/ppermute | solution.py:25
  37.3 16.8 %collective-permute-done = bf16[24,64,256]{2,0,1:T(8,128)(2,1)S(1)} collective-permute-done((bf16[24,64,256]{2,0,1:T(8,128)(2,1)S(1)}, bf16[24,64,256]{2,0,1:T(8,128)(2,1)S(1)}, u32[]{:S(2)}, u32[]{:S(2)}) %collective-permute-start) | collective-permute-done | bytes 786464 | tf_op jit(solution)/shard_map/ppermute | solution.py:25
  55.1 3.4 %collective-permute-start.3 = (bf16[12,64,256]{2,0,1:T(8,128)(2,1)}, bf16[12,64,256]{2,0,1:T(8,128)(2,1)}, u32[]{:S(2)}, u32[]{:S(2)}) collective-permute-start(bf16[12,64,256]{2,0,1:T(8,128)(2,1)} %slice.11), channel_id=1, source_target_pairs={{0,3},{1,0},{2,1},{3,2},{4,7},{5,4},{6,5},{7,6},{8,11},{9,8},{10,9... | collective-permute-start | bytes 1179656 | tf_op jit(solution)/shard_map/ppermute | solution.py:28
  60.4 2.5 %copy.79 = bf16[24,64,256]{1,2,0:T(8,128)(2,1)} copy(bf16[24,64,256]{2,0,1:T(8,128)(2,1)} %copy-done.5) | data formatting | bytes 1572864 | tf_op jit(solution)/shard_map/convert_element_type | solution.py:66
  62.9 1.6 copy.97
  64.8 13.8 %dynamic_update_slice.12 = bf16[24,256,256]{1,2,0:T(8,128)(2,1)S(1)} dynamic-update-slice(bf16[24,256,256]{1,2,0:T(8,128)(2,1)S(1)} %broadcast_in_dim.18, bf16[24,64,256]{1,2,0:T(8,128)(2,1)} %copy.79, s32[]{:T(128)} %constant.65.clone.1, s32[]{:T(128)S(6)} %select_n.60, s32[]{:T(128)} %constant.65.clone.1) | dynamic-update-slice | bytes 1572868 | tf_op jit(solution)/shard_map/dynamic_update_slice | solution.py:34
  78.6 2.5 %copy.80 = bf16[24,64,256]{1,2,0:T(8,128)(2,1)} copy(bf16[24,64,256]{2,0,1:T(8,128)(2,1)} %copy-done.3) | data formatting | bytes 1572864 | tf_op jit(solution)/shard_map/ppermute | solution.py:25
  81.1 17.3 %dynamic_update_slice.13 = bf16[24,256,256]{1,2,0:T(8,128)(2,1)S(1)} dynamic-update-slice(bf16[24,256,256]{1,2,0:T(8,128)(2,1)S(1)} %dynamic_update_slice.12, bf16[24,64,256]{1,2,0:T(8,128)(2,1)} %copy.80, s32[]{:T(128)} %constant.65.clone.1, s32[]{:T(128)S(6)} %select_n.62, s32[]{:T(128)} %constant.65.clone.1) | dynamic-update-slice | bytes 1572868 | tf_op jit(solution)/shard_map/dynamic_update_slice | solution.py:34
  98.4 2.5 %copy.82 = bf16[24,64,256]{1,2,0:T(8,128)(2,1)} copy(bf16[24,64,256]{2,0,1:T(8,128)(2,1)} %copy-done.2) | data formatting | bytes 1572864 | tf_op jit(solution)/shard_map/ppermute | solution.py:24
  100.9 2.3 %pad_maximum_fusion = bf16[24,64,256]{2,0,1:T(8,128)(2,1)} fusion(bf16[12,64,256]{2,0,1:T(8,128)(2,1)} %collective-permute-done.3, bf16[12,64,256]{2,0,1:T(8,128)(2,1)} %collective-permute-done.2), kind=kLoop, calls=%fused_computation.30 | loop fusion | flops 1572864 | bytes 1572864 | tf_op jit(solution)/shard_map/concatenate | solution.py:29
  103.2 2.5 %copy.81 = bf16[24,64,256]{1,2,0:T(8,128)(2,1)} copy(bf16[24,64,256]{2,0,1:T(8,128)(2,1)} %pad_maximum_fusion) | data formatting | bytes 1572864 | tf_op jit(solution)/shard_map/concatenate | solution.py:29
  105.7 13.5 %dynamic_update_slice.14 = bf16[24,256,256]{1,2,0:T(8,128)(2,1)S(1)} dynamic-update-slice(bf16[24,256,256]{1,2,0:T(8,128)(2,1)S(1)} %dynamic_update_slice.13, bf16[24,64,256]{1,2,0:T(8,128)(2,1)} %copy.81, s32[]{:T(128)} %constant.65.clone.1, s32[]{:T(128)S(6)} %select_n.64, s32[]{:T(128)} %constant.65.clone.1) | dynamic-update-slice | bytes 1572868 | tf_op jit(solution)/shard_map/dynamic_update_slice | solution.py:34
  119.2 17.0 %dynamic_update_slice.15 = bf16[24,256,256]{1,2,0:T(8,128)(2,1)S(1)} dynamic-update-slice(bf16[24,256,256]{1,2,0:T(8,128)(2,1)S(1)} %dynamic_update_slice.14, bf16[24,64,256]{1,2,0:T(8,128)(2,1)} %copy.82, s32[]{:T(128)} %constant.65.clone.1, s32[]{:T(128)S(6)} %select_n.66, s32[]{:T(128)} %constant.65.clone.1) | dynamic-update-slice | bytes 1572868 | tf_op jit(solution)/shard_map/dynamic_update_slice | solution.py:34
  136.2 3.3 %fusion.32 = f32[24,64,256]{2,1,0:T(8,128)} fusion(bf16[24,64,256]{1,2,0:T(8,128)(2,1)} %copy.79, bf16[24,256,256]{1,2,0:T(8,128)(2,1)S(1)} %dynamic_update_slice.15), kind=kOutput, calls=%fused_computation.57 | convolution fusion | flops 201326592 | bytes 5505024 | tf_op jit(solution)/shard_map/kij,klj->kil/dot_general | solution.py:71
  140.6 1.1 fusion.11
  141.7 1.1 fusion.9
  142.8 5.8 %multiply_reduce_fusion = (f32[24]{0:T(128)}, f32[24,64,256]{2,1,0:T(8,128)}) fusion(f32[24,256,256]{2,1,0:T(8,128)S(1)} %bitcast.32, f32[24,64,256]{2,1,0:T(8,128)S(1)} %fusion.14, f32[24,64,256]{2,1,0:T(8,128)S(1)} %fusion.11, f32[24,256,64]{1,2,0:T(8,128)S(1)} %fusion.9), kind=kOutput, calls=%fused_computation.17 | convolution fusion | flops 1209532416 | bytes 12583008 | tf_op jit(solution)/shard_map/kij,kjl->kil/dot_general | solution.py:86
  148.6 9.4 %all-reduce = (f32[24]{0:T(128)}, f32[24]{0:T(128)}) all-reduce(f32[24]{0:T(128)} %get-tuple-element.40, f32[24]{0:T(128)} %get-tuple-element.37), channel_id=1, replica_groups=mesh['shard'=32,'tensor'=4] {'tensor'}, use_global_device_ids=true, to_apply=%region_4.5 | all-reduce | flops 48 | bytes 384 | tf_op jit(solution)/shard_map/psum | solution.py:87
  158.6 4.8 %fusion.31 = (bf16[24,64,256]{2,1,0:T(8,128)(2,1)S(1)}, f32[24,64,256]{2,1,0:T(8,128)}, f32[24,64,256]{2,1,0:T(8,128)}) fusion(f32[24,64,256]{2,1,0:T(8,128)} %param.19, f32[24,64,256]{2,1,0:T(8,128)} %get-tuple-element.41, f32[24]{0:T(128)S(1)} %multiply_multiply_fusion.1, f32[24,64,256]{2,1,0:T(8,128)} %param.18), kind=kLoop, calls=%fused_computation.56 | loop fusion | flops 2359296 | bytes 8650848 | tf_op jit(solution)/shard_map/convert_element_type | solution.py:97
  164.2 1.6 copy.94
  165.7 7.8 %all-to-all-start.1 = ((bf16[32,64,256]{2,1,0:T(8,128)(2,1)}), bf16[32,64,256]{2,1,0:T(8,128)(2,1)}, u32[]{:S(2)}, u32[]{:S(2)}) async-start(bf16[32,64,256]{2,1,0:T(8,128)(2,1)} %copy.94), calls=%async_computation.1 | async-start | bytes 2097152 | tf_op jit(solution)/shard_map/all_to_all | solution.py:101
  173.6 3.7 %fusion.6 = f32[24,64,256]{2,0,1:T(8,128)S(1)} fusion(f32[24,64,256]{2,1,0:T(8,128)} %fusion.32, f32[24,64,256]{2,1,0:T(8,128)} %param.13), kind=kLoop, calls=%fused_computation.13 | loop fusion | flops 1179648 | bytes 4718592 | tf_op jit(solution)/shard_map/add | solution.py:71
  177.3 1.6 copy.95
  178.9 1.1 fusion.16
  180.3 1.8 fusion.5
  182.1 1.6 copy.96
  183.8 6.8 %all-to-all-done.1 = bf16[32,64,256]{2,1,0:T(8,128)(2,1)} async-done(((bf16[32,64,256]{2,1,0:T(8,128)(2,1)}), bf16[32,64,256]{2,1,0:T(8,128)(2,1)}, u32[]{:S(2)}, u32[]{:S(2)}) %all-to-all-start.1) | async-done | bytes 1048608 | tf_op jit(solution)/shard_map/all_to_all | solution.py:101
  190.6 1.8 gather_fusion
  (43 shorter events, 9.0 us)
Async XLA Ops:
  0.6 1.4 copy-start
  2.6 10.2 %copy-start.6 = (s32[384]{0:T(512)S(1)}, s32[384]{0:T(512)}, u32[]{:S(2)}) copy-start(s32[384]{0:T(512)} %param.12) | copy-start | bytes 4612
  4.1 25.5 %all-to-all-start = ((bf16[32,64,256]{2,1,0:T(8,128)(2,1)}), bf16[32,64,256]{2,1,0:T(8,128)(2,1)S(1)}, u32[]{:S(2)}, u32[]{:S(2)}) async-start(bf16[32,64,256]{2,1,0:T(8,128)(2,1)} %copy.77), calls=%async_computation | async-start | bytes 2097152 | tf_op jit(solution)/shard_map/all_to_all | solution.py:63
  33.5 26.7 %copy-start.5 = (bf16[24,64,256]{2,0,1:T(8,128)(2,1)}, bf16[24,64,256]{2,0,1:T(8,128)(2,1)S(1)}, u32[]{:S(2)}) copy-start(bf16[24,64,256]{2,0,1:T(8,128)(2,1)S(1)} %get-tuple-element.39) | copy-start | bytes 2359300
  33.5 20.5 %collective-permute-start = (bf16[24,64,256]{2,0,1:T(8,128)(2,1)S(1)}, bf16[24,64,256]{2,0,1:T(8,128)(2,1)S(1)}, u32[]{:S(2)}, u32[]{:S(2)}) collective-permute-start(bf16[24,64,256]{2,0,1:T(8,128)(2,1)S(1)} %get-tuple-element.39), channel_id=1, source_target_pairs={{0,3},{1,0},{2,1},{3,2},{4,7},{5,4},{6,5},{7,6},{8,11},{9,8},{10,9... | collective-permute-start | bytes 2359304 | tf_op jit(solution)/shard_map/ppermute | solution.py:25
  37.3 21.2 %collective-permute-start.1 = (bf16[24,64,256]{2,0,1:T(8,128)(2,1)S(1)}, bf16[24,64,256]{2,0,1:T(8,128)(2,1)S(1)}, u32[]{:S(2)}, u32[]{:S(2)}) collective-permute-start(bf16[24,64,256]{2,0,1:T(8,128)(2,1)S(1)} %get-tuple-element.39), channel_id=1, source_target_pairs={{0,1},{1,2},{2,3},{3,0},{4,5},{5,6},{6,7},{7,4},{8,9},{9,10},{10,1... | collective-permute-start | bytes 2359304 | tf_op jit(solution)/shard_map/ppermute | solution.py:24
  54.1 6.2 %copy-start.3 = (bf16[24,64,256]{2,0,1:T(8,128)(2,1)}, bf16[24,64,256]{2,0,1:T(8,128)(2,1)S(1)}, u32[]{:S(2)}) copy-start(bf16[24,64,256]{2,0,1:T(8,128)(2,1)S(1)} %collective-permute-done) | copy-start | bytes 2359300
  55.1 45.7 %collective-permute-start.3 = (bf16[12,64,256]{2,0,1:T(8,128)(2,1)}, bf16[12,64,256]{2,0,1:T(8,128)(2,1)}, u32[]{:S(2)}, u32[]{:S(2)}) collective-permute-start(bf16[12,64,256]{2,0,1:T(8,128)(2,1)} %slice.11), channel_id=1, source_target_pairs={{0,3},{1,0},{2,1},{3,2},{4,7},{5,4},{6,5},{7,6},{8,11},{9,8},{10,9... | collective-permute-start | bytes 1179656 | tf_op jit(solution)/shard_map/ppermute | solution.py:28
  58.5 0.9 copy-start.2
  60.3 40.6 %collective-permute-start.2 = (bf16[12,64,256]{2,0,1:T(8,128)(2,1)}, bf16[12,64,256]{2,0,1:T(8,128)(2,1)}, u32[]{:S(2)}, u32[]{:S(2)}) collective-permute-start(bf16[12,64,256]{2,0,1:T(8,128)(2,1)} %slice.10), channel_id=1, source_target_pairs={{0,1},{1,2},{2,3},{3,0},{4,5},{5,6},{6,7},{7,4},{8,9},{9,10},{10,1... | collective-permute-start | bytes 1179656 | tf_op jit(solution)/shard_map/ppermute | solution.py:27
  136.2 3.3 %copy-start.1 = (f32[24,64,256]{2,1,0:T(8,128)S(1)}, f32[24,64,256]{2,1,0:T(8,128)}, u32[]{:S(2)}) copy-start(f32[24,64,256]{2,1,0:T(8,128)} %param.15) | copy-start | bytes 4718596
  139.5 3.2 %slice-start = ((s8[6291456]{0:T(1024)(128)(4,1)}), s8[4194304]{0:T(1024)(128)(4,1)S(1)}, s32[]{:S(2)}) async-start(s8[6291456]{0:T(1024)(128)(4,1)} %bitcast.31), calls=%async_computation.2 | async-start | bytes 8388608
  140.6 2.2 %slice-start.1 = ((s8[6291456]{0:T(1024)(128)(4,1)}), s8[2097152]{0:T(1024)(128)(4,1)S(1)}, s32[]{:S(2)}) async-start(s8[6291456]{0:T(1024)(128)(4,1)} %bitcast.31), calls=%async_computation.3 | async-start | bytes 4194304
  165.7 24.9 %all-to-all-start.1 = ((bf16[32,64,256]{2,1,0:T(8,128)(2,1)}), bf16[32,64,256]{2,1,0:T(8,128)(2,1)}, u32[]{:S(2)}, u32[]{:S(2)}) async-start(bf16[32,64,256]{2,1,0:T(8,128)(2,1)} %copy.94), calls=%async_computation.1 | async-start | bytes 2097152 | tf_op jit(solution)/shard_map/all_to_all | solution.py:101
  178.9 1.4 copy-start.4
  182.1 10.3 %copy-start.7 = (pred[12]{0:T(512)(128)(4,1)S(1)}, pred[12]{0:T(512)(128)(4,1)}, u32[]{:S(2)}) copy-start(pred[12]{0:T(512)(128)(4,1)} %get-tuple-element.32) | copy-start | bytes 40

commit v2 on v1

--- a/solution.py
+++ b/solution.py
@@ -10,14 +10,6 @@
 eps_mean = 1e-06
 
 
-def split3(x):
-    hi = x.astype(jnp.bfloat16)
-    rest = x - hi.astype(jnp.float32)
-    mid = rest.astype(jnp.bfloat16)
-    lo = (rest - mid.astype(jnp.float32)).astype(jnp.bfloat16)
-    return hi, mid, lo
-
-
 def gather_rows(piece, splits, tensor_index):
     right = [(i, (i + 1) % splits) for i in range(splits)]
     left = [(i, (i - 1) % splits) for i in range(splits)]
@@ -27,12 +19,12 @@
     far_a = lax.ppermute(from_left[:half], "tensor", right)
     far_b = lax.ppermute(from_right[half:], "tensor", left)
     far = jnp.concatenate([far_a, far_b], 0)
-    rows = piece.shape[1]
-    whole = jnp.zeros((piece.shape[0], rows * splits, piece.shape[2]), piece.dtype)
-    for shift, part in ((0, piece), (1, from_right), (2, far), (splits - 1, from_left)):
-        start = ((tensor_index + shift) % splits) * rows
-        whole = lax.dynamic_update_slice_in_dim(whole, part, start, 1)
-    return whole
+    by_shift = (piece, from_right, far, from_left)
+
+    def ordered(first):
+        return lambda: jnp.concatenate([by_shift[(p - first) % splits] for p in range(splits)], 1)
+
+    return lax.switch(tensor_index, [ordered(first) for first in range(splits)])
 
 
 def on_device(
@@ -77,17 +69,16 @@
     grad_rows = grad_piece.astype(f32)
     second_new = beta_stat * moment + (1.0 - beta_stat) * grad_rows * grad_rows
     adam_step = grad_rows / (jnp.sqrt(second_new) + eps_root)
-    root_hi, root_mid, root_lo = split3(root_left)
-    precond = (
-        jnp.einsum("kij,kjl->kil", root_hi, grad_whole, preferred_element_type=f32)
-        + jnp.einsum("kij,kjl->kil", root_mid, grad_whole, preferred_element_type=f32)
-        + jnp.einsum("kij,kjl->kil", root_lo, grad_whole, preferred_element_type=f32)
+    precond = jnp.einsum("kij,kjl->kil", root_left, grad_whole.astype(f32), precision=highest)
+    precond = jnp.einsum("kij,kjl->kil", precond, root_right, precision=highest)
+    sums = jnp.stack(
+        [jnp.sum(adam_step * adam_step, axis=(1, 2)), jnp.sum(precond * precond, axis=(1, 2))]
     )
-    precond = jnp.einsum("kij,kjl->kil", precond, root_right, precision=highest)
-    adam_sum, precond_sum = lax.psum(
-        (jnp.sum(adam_step * adam_step, axis=(1, 2)), jnp.sum(precond * precond, axis=(1, 2))),
-        "tensor",
-    )
+    step = 1
+    while step < splits:
+        sums = sums + lax.ppermute(sums, "tensor", [(i, i ^ step) for i in range(splits)])
+        step *= 2
+    adam_sum, precond_sum = sums[0], sums[1]
     entries = float(rows_dev * splits * order)
     scale_ratio = jnp.sqrt(adam_sum / entries + eps_mean) / jnp.sqrt(
         precond_sum / entries + eps_mean

time: 195 us -> 126 us (0.65)
  local copies, waits for them, and re-layouts: 85.9 us -> 15 us
  waiting for transfers between devices: 40.2 us -> 50.8 us
  blocking collectives: 9.41 us -> 0 us
  other arithmetic: 14.8 us -> 10.8 us
  matrix products: 18.5 us -> 21.9 us
  starting transfers between devices: 23.5 us -> 25.8 us
    dynamic_update_slice x4 -> x0, local copies, waits for them, and re-layouts: 61.5 us -> none  [gather_rows(): whole = lax.dynamic_update_slice_in_dim(whole, part, start, 1)]
    ppermute x1, waiting for transfers between devices: 0.01 us -> 17.7 us  [gather_rows(): from_left = lax.ppermute(piece, 'tensor', right)]
    ppermute x1, waiting for transfers between devices: 16.8 us -> 0.01 us  [gather_rows(): from_right = lax.ppermute(piece, 'tensor', left)]
    ppermute x1, waiting for transfers between devices: 0.01 us -> 10.4 us  [gather_rows(): far_a = lax.ppermute(from_left[:half], 'tensor', right)]
    psum x1 -> x0, blocking collectives: 9.41 us -> none  [on_device(): lax.psum((jnp.sum(adam_step * adam_step, axis=(1, 2)), jnp.sum(precond *...]
    ppermute x2 -> x0, local copies, waits for them, and re-layouts: 5.01 us -> none  [the longest x1 2.5 us: gather_rows(): from_right = lax.ppermute(piece, 'tensor', left)]
    ppermute x0 -> x2, starting transfers between devices: none -> 4.65 us  [on_device(): lax.ppermute(sums, 'tensor', [(i, i ^ step) for i in range(splits)])]
    convert_element_type x1, other arithmetic: 4.81 us -> 2.23 us  [on_device(): weight_half = weight_new.astype(jnp.bfloat16)]
  transfers between devices with their start and end apart: 6 -> 8, of which waited for: 3 -> 5; matrix products, arithmetic and copies ran while one was open for 27% -> 14% of each run, Pallas kernels for 0% -> 0%
where the time goes in v2:
time: 126 us; the launch traced here: 125 us
  waiting for transfers between devices  50.8 us (40%)
  starting transfers between devices  25.8 us (20%)
  matrix products  21.9 us (17%)
  local copies, waits for them, and re-layouts  15 us (12%)
  other arithmetic  10.8 us (9%)
    ppermute x1, waiting for transfers between devices, gather_rows(): from_left = lax.ppermute(piece, 'tensor', right)  17.7 us
    all_to_all x1, waiting for transfers between devices, on_device(): lax.all_to_all(outgoing, 'shard', split_axis=0, concat_axis=0, tiled=True)  16.6 us
    ppermute x1, waiting for transfers between devices, gather_rows(): far_a = lax.ppermute(from_left[:half], 'tensor', right)  10.4 us
    all_to_all x1, starting transfers between devices, on_device(): lax.all_to_all(outgoing, 'shard', split_axis=0, concat_axis=0, tiled=True)  8.71 us
    dot_general x1, matrix products, on_device(): precond = jnp.einsum('kij,kjl->kil', precond, root_right, precision=highest)  7.9 us
    unnamed x27, local copies, waits for them, and re-layouts  7.47 us
    all_to_all x1, starting transfers between devices, on_device(): lax.all_to_all(returning, 'shard', split_axis=0, concat_axis=0, tiled=True)  5.97 us
    all_to_all x1, waiting for transfers between devices, on_device(): lax.all_to_all(returning, 'shard', split_axis=0, concat_axis=0, tiled=True)  5.94 us
  transfers between devices with their start and end apart: 8, of which 5 were waited for; matrix products, arithmetic and copies ran while one was open for 14% of the time, Pallas kernels for 0%

profile of v2, /device:TPU:1, one launch (start us, length us, event | category | flops | bytes accessed | tf_op | source)
XLA Modules:
  0.0 125.2 jit_solution(8016406494790249706)
XLA Ops:
  0.7 0.9 reshape.83
  1.6 1.6 %convolution_convert_fusion.1 = bf16[32,64,256]{2,0,1:T(8,128)(2,1)S(1)} fusion(bf16[12,64,256]{2,1,0:T(8,128)(2,1)} %param.14, s32[12]{0:T(128)S(1)} %get-tuple-element.148), kind=kOutput, calls=%fused_computation.23 | convolution fusion | flops 13107584 | bytes 1441840 | tf_op jit(solution)/shard_map/gi,ixy->gxy/dot_general | solution.py:52
  3.1 1.6 %copy.107 = bf16[32,64,256]{2,1,0:T(8,128)(2,1)} copy(bf16[32,64,256]{2,0,1:T(8,128)(2,1)S(1)} %convolution_convert_fusion.1) | data formatting | bytes 2097152 | tf_op jit(solution)/shard_map/convert_element_type | solution.py:54
  4.7 8.7 %all-to-all-start = ((bf16[32,64,256]{2,1,0:T(8,128)(2,1)}), bf16[32,64,256]{2,1,0:T(8,128)(2,1)S(1)}, u32[]{:S(2)}, u32[]{:S(2)}) async-start(bf16[32,64,256]{2,1,0:T(8,128)(2,1)} %copy.107), calls=%async_computation | async-start | bytes 2097152 | tf_op jit(solution)/shard_map/all_to_all | solution.py:55
  13.8 16.6 %all-to-all-done = bf16[32,64,256]{2,1,0:T(8,128)(2,1)S(1)} async-done(((bf16[32,64,256]{2,1,0:T(8,128)(2,1)}), bf16[32,64,256]{2,1,0:T(8,128)(2,1)S(1)}, u32[]{:S(2)}, u32[]{:S(2)}) %all-to-all-start) | async-done | bytes 1048608 | tf_op jit(solution)/shard_map/all_to_all | solution.py:55
  30.3 4.5 %fusion.6 = (f32[24]{0:T(128)S(1)}, f32[24,64,256]{2,0,1:T(8,128)}, bf16[24,64,256]{2,0,1:T(8,128)(2,1)S(1)}) fusion(f32[24,64,256]{2,1,0:T(8,128)} %param.21, bf16[32,64,256]{2,1,0:T(8,128)(2,1)S(1)} %all-to-all-done, s32[24,32]{1,0:T(8,128)S(1)} %convert_reduce_fusion), kind=kOutput, calls=%fused_computation.21 | convolution fusion | flops 29098728 | bytes 4983904 | tf_op jit(solution)/shard_map/kg,gxy->kxy/dot_general | solution.py:56
  34.8 1.7 %collective-permute-start.1 = (bf16[24,64,256]{2,0,1:T(8,128)(2,1)S(1)}, bf16[24,64,256]{2,0,1:T(8,128)(2,1)S(1)}, u32[]{:S(2)}, u32[]{:S(2)}) collective-permute-start(bf16[24,64,256]{2,0,1:T(8,128)(2,1)S(1)} %get-tuple-element.154), channel_id=1, source_target_pairs={{0,1},{1,2},{2,3},{3,0},{4,5},{5,6},{6,7},{7,4},{8,9},{9,10},{10,1... | collective-permute-start | bytes 2359304 | tf_op jit(solution)/shard_map/ppermute | solution.py:16
  36.5 2.2 %collective-permute-start = (bf16[24,64,256]{2,0,1:T(8,128)(2,1)S(1)}, bf16[24,64,256]{2,0,1:T(8,128)(2,1)S(1)}, u32[]{:S(2)}, u32[]{:S(2)}) collective-permute-start(bf16[24,64,256]{2,0,1:T(8,128)(2,1)S(1)} %get-tuple-element.154), channel_id=1, source_target_pairs={{0,3},{1,0},{2,1},{3,2},{4,7},{5,4},{6,5},{7,6},{8,11},{9,8},{10,9... | collective-permute-start | bytes 2359304 | tf_op jit(solution)/shard_map/ppermute | solution.py:17
  38.7 17.7 %collective-permute-done.1 = bf16[24,64,256]{2,0,1:T(8,128)(2,1)S(1)} collective-permute-done((bf16[24,64,256]{2,0,1:T(8,128)(2,1)S(1)}, bf16[24,64,256]{2,0,1:T(8,128)(2,1)S(1)}, u32[]{:S(2)}, u32[]{:S(2)}) %collective-permute-start.1) | collective-permute-done | bytes 786464 | tf_op jit(solution)/shard_map/ppermute | solution.py:16
  56.4 0.9 slice.18
  57.5 1.0 slice.19
  58.5 2.5 %collective-permute-start.3 = (bf16[12,64,256]{2,0,1:T(8,128)(2,1)}, bf16[12,64,256]{2,0,1:T(8,128)(2,1)S(1)}, u32[]{:S(2)}, u32[]{:S(2)}) collective-permute-start(bf16[12,64,256]{2,0,1:T(8,128)(2,1)} %slice.19), channel_id=1, source_target_pairs={{0,3},{1,0},{2,1},{3,2},{4,7},{5,4},{6,5},{7,6},{8,11},{9,8},{10,9... | collective-permute-start | bytes 1179656 | tf_op jit(solution)/shard_map/ppermute | solution.py:20
  61.1 10.4 %collective-permute-done.2 = bf16[12,64,256]{2,0,1:T(8,128)(2,1)S(1)} collective-permute-done((bf16[12,64,256]{2,0,1:T(8,128)(2,1)}, bf16[12,64,256]{2,0,1:T(8,128)(2,1)S(1)}, u32[]{:S(2)}, u32[]{:S(2)}) %collective-permute-start.2) | collective-permute-done | bytes 393248 | tf_op jit(solution)/shard_map/ppermute | solution.py:19
  72.0 2.5 %conditional.1 = (bf16[24,256,256]{2,1,0:T(8,128)(2,1)}) conditional(s32[]{:T(128)} %clamp.3, (bf16[24,64,256]{2,0,1:T(8,128)(2,1)S(1)}, bf16[24,64,256]{2,0,1:T(8,128)(2,1)S(1)}, bf16[24,64,256]{2,0,1:T(8,128)(2,1)S(1)}, bf16[24,64,256]{2,0,1:T(8,128)(2,1)S(1)}) %tuple.59, (bf16[24,64,256]{2,0,1:T(8,128)(2,1)S(1)}, ...), branch_computations={%region_1.2_spmd, %region_2.3_spmd, %region_3.4_spmd, %region_4.5_... | conditional | flops 12582912 | bytes 12582920 | solution.py:27
  72.7 1.8 %pad_maximum_fusion = bf16[24,256,256]{2,1,0:T(8,128)(2,1)} fusion(bf16[24,64,256]{2,1,0:T(8,128)(2,1)S(1)} %copy.112, bf16[24,64,256]{2,1,0:T(8,128)(2,1)S(1)} %copy.111, bf16[24,64,256]{2,1,0:T(8,128)(2,1)S(1)} %copy.110, bf16[24,64,256]{2,1,0:T(8,128)(2,1)S(1)} %copy.109), kind=kLoop, calls=%fused_computation.1 | loop fusion | flops 12582912 | bytes 6291456 | tf_op jit(solution)/shard_map/cond/branch_0_fun/concatenate | solution.py:25
  74.5 3.7 %fusion.26 = f32[24,256,64]{1,2,0:T(8,128)S(1)} fusion(bf16[24,256,256]{2,1,0:T(8,128)(2,1)} %get-tuple-element.157, f32[24,64,256]{2,1,0:T(8,128)S(1)} %copy-done), kind=kOutput, calls=%fused_computation.55 | convolution fusion | flops 1207959552 | bytes 6291456 | tf_op jit(solution)/shard_map/kij,kjl->kil/dot_general | solution.py:72
  78.2 7.9 %multiply_reduce_fusion = (f32[24]{0:T(128)S(1)}, f32[24,64,256]{2,1,0:T(8,128)}) fusion(f32[24,256,64]{1,2,0:T(8,128)S(1)} %fusion.26, f32[24,256,256]{2,1,0:T(8,128)} %param.20), kind=kOutput, calls=%fused_computation.18 | convolution fusion | flops 1208745984 | bytes 9437280 | tf_op jit(solution)/shard_map/kij,kjl->kil/dot_general | solution.py:73
  86.2 3.2 %copy.135 = f32[24,64,256]{2,1,0:T(8,128)} copy(f32[24,64,256]{2,0,1:T(8,128)} %get-tuple-element.153) | data formatting | bytes 3145728
  89.4 4.6 %collective-permute-start.5 = (f32[2,24]{1,0:T(2,128)S(1)}, f32[2,24]{1,0:T(2,128)S(1)}, u32[]{:S(2)}, u32[]{:S(2)}) collective-permute-start(f32[2,24]{1,0:T(2,128)S(1)} %fusion.23), channel_id=1, source_target_pairs={{0,2},{1,3},{2,0},{3,1},{4,6},{5,7},{6,4},{7,5},{8,10},{9,11},{10,... | collective-permute-start | bytes 584 | tf_op jit(solution)/shard_map/ppermute | solution.py:79
  94.0 2.2 %fusion.9 = f32[24,64,256]{2,1,0:T(8,128)} fusion(bf16[24,256,256]{2,1,0:T(8,128)(2,1)S(1)} %copy-done.1, bf16[24,64,256]{2,0,1:T(8,128)(2,1)S(1)} %get-tuple-element.154), kind=kOutput, calls=%fused_computation.28 | convolution fusion | flops 201326592 | bytes 5505024 | tf_op jit(solution)/shard_map/kij,klj->kil/dot_general | solution.py:63
  96.3 2.2 %fusion.25 = (bf16[24,64,256]{2,1,0:T(8,128)(2,1)S(1)}, f32[24,64,256]{2,1,0:T(8,128)}, f32[24,64,256]{2,1,0:T(8,128)}) fusion(f32[24,64,256]{2,1,0:T(8,128)S(1)} %copy-done.9, f32[24,64,256]{2,1,0:T(8,128)S(1)} %copy-done.7, f32[24]{0:T(128)S(1)} %multiply_bitcast_fusion, f32[24,64,256]{2,1,0:T(8,128)S(1)} %copy-done.10), kind=kLoop, calls=%fused_computation.54 | loop fusion | flops 2359296 | bytes 8650848 | tf_op jit(solution)/shard_map/convert_element_type | solution.py:88
  98.5 0.7 convolution_convert_fusion
  99.2 1.6 %copy.132 = bf16[32,64,256]{2,1,0:T(8,128)(2,1)} copy(bf16[32,64,256]{2,0,1:T(8,128)(2,1)S(1)} %convolution_convert_fusion) | data formatting | bytes 2097152 | tf_op jit(solution)/shard_map/convert_element_type | solution.py:91
  100.8 6.0 %all-to-all-start.1 = ((bf16[32,64,256]{2,1,0:T(8,128)(2,1)}), bf16[32,64,256]{2,1,0:T(8,128)(2,1)S(1)}, u32[]{:S(2)}, u32[]{:S(2)}) async-start(bf16[32,64,256]{2,1,0:T(8,128)(2,1)} %copy.132), calls=%async_computation.1 | async-start | bytes 2097152 | tf_op jit(solution)/shard_map/all_to_all | solution.py:92
  106.7 3.7 %fusion.3 = f32[24,64,256]{2,0,1:T(8,128)S(1)} fusion(f32[24,64,256]{2,1,0:T(8,128)} %fusion.9, f32[24,64,256]{2,1,0:T(8,128)} %param.17), kind=kLoop, calls=%fused_computation.14 | loop fusion | flops 1179648 | bytes 4718592 | tf_op jit(solution)/shard_map/add | solution.py:63
  110.5 1.6 %copy.133 = f32[24,64,256]{2,1,0:T(8,128)} copy(f32[24,64,256]{2,0,1:T(8,128)S(1)} %fusion.3) | data formatting | bytes 3145728
  112.1 0.8 copy-done.2
  112.9 1.4 %fusion.4 = f32[24,64,256]{2,1,0:T(8,128)S(1)} fusion(bf16[24,256,256]{2,1,0:T(8,128)(2,1)S(1)} %copy-done.2, s32[]{:T(128)S(6)} %select_n.28), kind=kOutput, calls=%fused_computation.19 | convolution fusion | flops 201326592 | bytes 6291460 | tf_op jit(solution)/shard_map/kji,kjl->kil/dot_general | solution.py:66
  114.3 1.8 %fusion.2 = f32[24,64,256]{2,0,1:T(8,128)S(1)} fusion(f32[24,64,256]{2,1,0:T(8,128)S(1)} %fusion.4, f32[24,64,256]{2,1,0:T(8,128)S(1)} %copy-done.8), kind=kLoop, calls=%fused_computation.11 | loop fusion | flops 1179648 | bytes 4718592 | tf_op jit(solution)/shard_map/add | solution.py:66
  116.2 1.6 %copy.134 = f32[24,64,256]{2,1,0:T(8,128)} copy(f32[24,64,256]{2,0,1:T(8,128)S(1)} %fusion.2) | data formatting | bytes 3145728
  117.8 5.9 %all-to-all-done.1 = bf16[32,64,256]{2,1,0:T(8,128)(2,1)S(1)} async-done(((bf16[32,64,256]{2,1,0:T(8,128)(2,1)}), bf16[32,64,256]{2,1,0:T(8,128)(2,1)S(1)}, u32[]{:S(2)}, u32[]{:S(2)}) %all-to-all-start.1) | async-done | bytes 1048608 | tf_op jit(solution)/shard_map/all_to_all | solution.py:92
  124.3 0.9 broadcast_select_fusion
  (47 shorter events, 2.3 us)
Async XLA Ops:
  0.6 73.8 %copy-start = (f32[24,64,256]{2,1,0:T(8,128)S(1)}, f32[24,64,256]{2,1,0:T(8,128)}, u32[]{:S(2)}) copy-start(f32[24,64,256]{2,1,0:T(8,128)} %param.19) | copy-start | bytes 4718596
  4.7 8.8 %copy-start.11 = (s32[384]{0:T(512)S(1)}, s32[384]{0:T(512)}, u32[]{:S(2)}) copy-start(s32[384]{0:T(512)} %param.16) | copy-start | bytes 4612
  4.7 25.6 %all-to-all-start = ((bf16[32,64,256]{2,1,0:T(8,128)(2,1)}), bf16[32,64,256]{2,1,0:T(8,128)(2,1)S(1)}, u32[]{:S(2)}, u32[]{:S(2)}) async-start(bf16[32,64,256]{2,1,0:T(8,128)(2,1)} %copy.107), calls=%async_computation | async-start | bytes 2097152 | tf_op jit(solution)/shard_map/all_to_all | solution.py:55
  34.8 21.6 %collective-permute-start.1 = (bf16[24,64,256]{2,0,1:T(8,128)(2,1)S(1)}, bf16[24,64,256]{2,0,1:T(8,128)(2,1)S(1)}, u32[]{:S(2)}, u32[]{:S(2)}) collective-permute-start(bf16[24,64,256]{2,0,1:T(8,128)(2,1)S(1)} %get-tuple-element.154), channel_id=1, source_target_pairs={{0,1},{1,2},{2,3},{3,0},{4,5},{5,6},{6,7},{7,4},{8,9},{9,10},{10,1... | collective-permute-start | bytes 2359304 | tf_op jit(solution)/shard_map/ppermute | solution.py:16
  36.5 20.8 %collective-permute-start = (bf16[24,64,256]{2,0,1:T(8,128)(2,1)S(1)}, bf16[24,64,256]{2,0,1:T(8,128)(2,1)S(1)}, u32[]{:S(2)}, u32[]{:S(2)}) collective-permute-start(bf16[24,64,256]{2,0,1:T(8,128)(2,1)S(1)} %get-tuple-element.154), channel_id=1, source_target_pairs={{0,3},{1,0},{2,1},{3,2},{4,7},{5,4},{6,5},{7,6},{8,11},{9,8},{10,9... | collective-permute-start | bytes 2359304 | tf_op jit(solution)/shard_map/ppermute | solution.py:17
  56.4 1.1 copy-start.3
  57.3 14.2 %collective-permute-start.2 = (bf16[12,64,256]{2,0,1:T(8,128)(2,1)}, bf16[12,64,256]{2,0,1:T(8,128)(2,1)S(1)}, u32[]{:S(2)}, u32[]{:S(2)}) collective-permute-start(bf16[12,64,256]{2,0,1:T(8,128)(2,1)} %slice.18), channel_id=1, source_target_pairs={{0,1},{1,2},{2,3},{3,0},{4,5},{5,6},{6,7},{7,4},{8,9},{9,10},{10,1... | collective-permute-start | bytes 1179656 | tf_op jit(solution)/shard_map/ppermute | solution.py:19
  57.5 1.1 copy-start.5
  58.5 13.2 %collective-permute-start.3 = (bf16[12,64,256]{2,0,1:T(8,128)(2,1)}, bf16[12,64,256]{2,0,1:T(8,128)(2,1)S(1)}, u32[]{:S(2)}, u32[]{:S(2)}) collective-permute-start(bf16[12,64,256]{2,0,1:T(8,128)(2,1)} %slice.19), channel_id=1, source_target_pairs={{0,3},{1,0},{2,1},{3,2},{4,7},{5,4},{6,5},{7,6},{8,11},{9,8},{10,9... | collective-permute-start | bytes 1179656 | tf_op jit(solution)/shard_map/ppermute | solution.py:20
  61.1 10.9 %copy-start.4 = (bf16[24,64,256]{2,0,1:T(8,128)(2,1)S(1)}, bf16[24,64,256]{2,0,1:T(8,128)(2,1)}, u32[]{:S(2)}) copy-start(bf16[24,64,256]{2,0,1:T(8,128)(2,1)} %copy-done.3) | copy-start | bytes 2359300
  61.1 10.9 %copy-start.6 = (bf16[24,64,256]{2,0,1:T(8,128)(2,1)S(1)}, bf16[24,64,256]{2,0,1:T(8,128)(2,1)}, u32[]{:S(2)}) copy-start(bf16[24,64,256]{2,0,1:T(8,128)(2,1)} %copy-done.5) | copy-start | bytes 2359300
  86.1 3.3 %collective-permute-start.4 = (f32[2,24]{1,0:T(2,128)S(1)}, f32[2,24]{1,0:T(2,128)S(1)}, u32[]{:S(2)}, u32[]{:S(2)}) collective-permute-start(f32[2,24]{1,0:T(2,128)S(1)} %pad_maximum_fusion.5), channel_id=1, source_target_pairs={{0,1},{1,0},{2,3},{3,2},{4,5},{5,4},{6,7},{7,6},{8,9},{9,8},{10,11... | collective-permute-start | bytes 584 | tf_op jit(solution)/shard_map/ppermute | solution.py:79
  86.2 7.8 %copy-start.1 = (bf16[24,256,256]{2,1,0:T(8,128)(2,1)S(1)}, bf16[24,256,256]{2,1,0:T(8,128)(2,1)}, u32[]{:S(2)}) copy-start(bf16[24,256,256]{2,1,0:T(8,128)(2,1)} %get-tuple-element.157) | copy-start | bytes 9437188
  89.4 6.8 %copy-start.7 = (f32[24,64,256]{2,1,0:T(8,128)S(1)}, f32[24,64,256]{2,1,0:T(8,128)}, u32[]{:S(2)}) copy-start(f32[24,64,256]{2,1,0:T(8,128)} %get-tuple-element.156) | copy-start | bytes 4718596
  89.4 6.8 %copy-start.9 = (f32[24,64,256]{2,1,0:T(8,128)S(1)}, f32[24,64,256]{2,1,0:T(8,128)}, u32[]{:S(2)}) copy-start(f32[24,64,256]{2,1,0:T(8,128)} %param.23) | copy-start | bytes 4718596
  89.4 6.8 %copy-start.10 = (f32[24,64,256]{2,1,0:T(8,128)S(1)}, f32[24,64,256]{2,1,0:T(8,128)}, u32[]{:S(2)}) copy-start(f32[24,64,256]{2,1,0:T(8,128)} %param.22) | copy-start | bytes 4718596
  89.4 6.8 %collective-permute-start.5 = (f32[2,24]{1,0:T(2,128)S(1)}, f32[2,24]{1,0:T(2,128)S(1)}, u32[]{:S(2)}, u32[]{:S(2)}) collective-permute-start(f32[2,24]{1,0:T(2,128)S(1)} %fusion.23), channel_id=1, source_target_pairs={{0,2},{1,3},{2,0},{3,1},{4,6},{5,7},{6,4},{7,5},{8,10},{9,11},{10,... | collective-permute-start | bytes 584 | tf_op jit(solution)/shard_map/ppermute | solution.py:79
  100.8 23.0 %all-to-all-start.1 = ((bf16[32,64,256]{2,1,0:T(8,128)(2,1)}), bf16[32,64,256]{2,1,0:T(8,128)(2,1)S(1)}, u32[]{:S(2)}, u32[]{:S(2)}) async-start(bf16[32,64,256]{2,1,0:T(8,128)(2,1)} %copy.132), calls=%async_computation.1 | async-start | bytes 2097152 | tf_op jit(solution)/shard_map/all_to_all | solution.py:92
  110.5 2.5 %copy-start.2 = (bf16[24,256,256]{2,1,0:T(8,128)(2,1)S(1)}, bf16[24,256,256]{2,1,0:T(8,128)(2,1)}, u32[]{:S(2)}) copy-start(bf16[24,256,256]{2,1,0:T(8,128)(2,1)} %get-tuple-element.157) | copy-start | bytes 9437188
  112.9 1.4 %copy-start.8 = (f32[24,64,256]{2,1,0:T(8,128)S(1)}, f32[24,64,256]{2,1,0:T(8,128)}, u32[]{:S(2)}) copy-start(f32[24,64,256]{2,1,0:T(8,128)} %param.18) | copy-start | bytes 4718596
